TPU v7x, 32 devices: a whole 2x2x4 slice. The times are simulated.
32 devices in a mesh: groups: 2 (over x), wide: 4 (over y, core), expert: 4 (over z).
Axes of the slice: x: 2, y: 2, z: 4, core: 2. Of those that a mesh axis runs over, the one named last changes fastest.
Arguments:
- prompts: bfloat16 [8, 128, 6144], P(('groups', 'wide'), None, 'expert'), parts along dimension 0, may hold values from -6 to 6
- span_slot_owner: int32 [8], P('groups'), parts along dimension 0, may hold values from 0 to 3, as said below
- row_expert_index: int32 [768, 2], P('groups'), parts along dimension 0, may hold values from 0 to 7, all different within a row
- tile_tenant_index: int32 [6], P('groups'), parts along dimension 0, may hold values from 0 to 7
- tenant_adapter_slot: int32 [16], P('groups'), parts along dimension 0, may hold values from 0 to 7, each once
- router: bfloat16 [6144, 8], replicated, may hold values from -0.078125 to 0.078125
- gate_weight: bfloat16 [2, 6144, 16384], P(None, None, ('wide', 'expert')), may hold values from -0.078125 to 0.078125
- up_weight: bfloat16 [2, 6144, 16384], P(None, None, ('wide', 'expert')), may hold values from -0.078125 to 0.078125
- down_weight: bfloat16 [2, 16384, 6144], P(None, 'wide', 'expert'), may hold values from -0.046875 to 0.046875
- adapter_down_weight: bfloat16 [16, 2, 6144, 64], P(('groups', 'wide'), None, 'expert'), parts along dimension 0, may hold values from -0.078125 to 0.078125
- adapter_up_weight: bfloat16 [16, 2, 64, 16384], P('groups', None, None, ('wide', 'expert')), parts along dimension 0, may hold values from -0.75 to 0.75
Outputs:
- mixed: bfloat16 [768, 6144], P(('groups', 'wide'), 'expert'), parts along dimension 0
There are 2 independent parts, one for each index of `groups`. A program takes and returns all parts, laid end to end along the dimension named above; an argument that names none is the same for every part. Nothing has to cross between parts.
Inputs may be any that keep to these rules, and one draw needn't show every extreme that they name: `span_slot_owner`: a permutation of the slots; span c, for c < 3, is in slot span_slot_owner[c]. `row_expert_index`: each row names two different experts. `tenant_adapter_slot`: a permutation of the slots. `tile_tenant_index`: tenant of rows 128 * i to 128 * i + 127.
All inputs are finite; a program needn't handle non-finite values.
Results may differ from a plain program's by a relative error of at most 0.0051.
Values may be sent and summed in bfloat16 or wider, within the bound.
No kernel may reach another device: no remote copies, remote signals or barrier semaphores. Data moves between devices by JAX's collectives and lax.ppermute only.
A program may use at most 128 MiB of HBM per device.

v0:
```python
import jax
import jax.numpy as jnp
import numpy as np
from jax import lax
from jax.sharding import Mesh
from jax.sharding import PartitionSpec as P

ADAPTER_SCALE = 0.5
WIDE = ("wy", "wc")
GROUP = ("wy", "wc", "expert")


def per_device(
    prompts,
    span_slot_owner,
    row_expert_index,
    tile_tenant_index,
    tenant_adapter_slot,
    router,
    gate_weight,
    up_weight,
    down_weight,
    adapter_down_weight,
    adapter_up_weight,
):
    span = prompts.shape[1]
    quarter = prompts.shape[2]
    tokens = row_expert_index.shape[0]
    nchunk = tokens // span
    window = gate_weight.shape[0]
    core = lax.axis_index("wc")
    cores = lax.axis_size("wc")
    wide_index = lax.axis_index(WIDE)
    slots_q = lax.all_gather(prompts, WIDE, axis=0, tiled=True)
    rows_q = jnp.take(slots_q, span_slot_owner[:nchunk], axis=0).reshape(tokens, quarter)
    half = tokens // cores
    mine_q = lax.dynamic_slice_in_dim(rows_q, core * half, half, 0)
    mine = lax.all_gather(mine_q, "expert", axis=1, tiled=True)
    other = lax.ppermute(mine, "wc", [(i, (i + 1) % cores) for i in range(cores)])
    first = jnp.where(core == 0, mine, other)
    second = jnp.where(core == 0, other, mine)
    input_rows = jnp.concatenate([first, second], axis=0)
    logits = jnp.dot(input_rows, router, preferred_element_type=jnp.float32)
    experts = jnp.arange(router.shape[1], dtype=jnp.int32)
    picked = (row_expert_index[:, :, None] == experts[None, None, :]).astype(jnp.float32)
    chosen = jnp.sum(picked * logits[:, None, :], axis=2)
    first_prob = jax.nn.sigmoid(chosen[:, 0] - chosen[:, 1])
    second_prob = jax.nn.sigmoid(chosen[:, 1] - chosen[:, 0])
    weight = (
        first_prob[:, None] * picked[:, 0, :window] + second_prob[:, None] * picked[:, 1, :window]
    )
    tile_count = tile_tenant_index.shape[0]
    tile_rows = tokens // tile_count
    resident_slots = adapter_down_weight.shape[0]
    tile_slot_index = jnp.take(tenant_adapter_slot, tile_tenant_index)
    owners = tile_slot_index // resident_slots
    local_index = tile_slot_index % resident_slots
    held = jnp.take(adapter_down_weight, local_index, axis=0)
    partial_rank = jnp.einsum(
        "ntd,nedr->nter",
        rows_q.reshape(tile_count, tile_rows, quarter),
        held,
        preferred_element_type=jnp.float32,
    )
    partial_rank = jnp.where(
        (owners == wide_index)[:, None, None, None], partial_rank, jnp.zeros_like(partial_rank)
    )
    lowrank = lax.reduce_precision(lax.psum(partial_rank, GROUP), exponent_bits=8, mantissa_bits=7)
    tile_up = jnp.take(adapter_up_weight, tile_tenant_index, axis=0)
    adapted_hidden = jnp.einsum(
        "nter,nerf->ntef", lowrank, tile_up.astype(jnp.float32), preferred_element_type=jnp.float32
    ).reshape(tokens, window, tile_up.shape[3])
    running = None
    for expert_number in range(window):
        gate_pre = jnp.dot(
            input_rows, gate_weight[expert_number], preferred_element_type=jnp.float32
        )
        up_value = (
            jnp.dot(input_rows, up_weight[expert_number], preferred_element_type=jnp.float32)
            + ADAPTER_SCALE * adapted_hidden[:, expert_number]
        )
        hidden = (weight[:, expert_number, None] * jax.nn.silu(gate_pre) * up_value).astype(
            jnp.bfloat16
        )
        gathered = lax.all_gather(hidden, "expert", axis=1, tiled=True)
        part = jnp.dot(gathered, down_weight[expert_number], preferred_element_type=jnp.float32)
        running = part if running is None else running + part
    mixed_rows = lax.psum_scatter(running, WIDE, scatter_dimension=0, tiled=True)
    return mixed_rows.astype(jnp.bfloat16)


def solution(mesh):
    groups = mesh.shape["groups"]
    wide = mesh.shape["wide"]
    expert = mesh.shape["expert"]
    split = Mesh(
        np.asarray(mesh.devices).reshape(groups, wide // 2, 2, expert),
        ("groups", "wy", "wc", "expert"),
    )
    rows = ("groups", "wy", "wc")
    in_specs = (
        P(rows, None, "expert"),
        P("groups"),
        P("groups", None),
        P("groups"),
        P("groups"),
        P(),
        P(None, None, GROUP),
        P(None, None, GROUP),
        P(None, WIDE, "expert"),
        P(rows, None, "expert", None),
        P("groups", None, None, GROUP),
    )
    out_specs = P(rows, "expert")
    return jax.shard_map(
        per_device, mesh=split, in_specs=in_specs, out_specs=out_specs, check_vma=False
    )
```

profile of v0, /device:TPU:0, one launch (start us, length us, event | category | flops | bytes accessed | tf_op | source)
XLA Modules:
  0.0 382.7 jit_solution(16340851096399354820)
XLA Ops:
  6.5 0.7 all-gather.5.cloned.1.call-update
  7.3 0.7 compare_and_fusion.2
  8.1 23.2 %all-gather.5.cloned.1.call-done = bf16[4,128,1536]{2,1,0:T(8,128)(2,1)} async-done(((bf16[1,128,1536]{2,1,0:T(8,128)(2,1)}), bf16[4,128,1536]{2,1,0:T(8,128)(2,1)}) %all-gather.5.cloned.1.call-update) | async-done | bytes 1572880 | tf_op jit(solution)/shard_map/all_gather | solution.py:34
  31.3 2.0 gather_fusion
  33.4 1.1 dynamic-slice_select_fusion
  34.6 50.6 %all-gather.7.cloned.1.call-done = bf16[192,6144]{1,0:T(8,128)(2,1)} async-done(((bf16[192,1536]{1,0:T(8,128)(2,1)}), bf16[192,6144]{1,0:T(8,128)(2,1)}) %all-gather.7.cloned.1.call-update) | async-done | bytes 2359312 | tf_op jit(solution)/shard_map/all_gather | solution.py:38
  85.9 1.8 gather_fusion.3
  87.8 1.1 copy-done.6
  89.5 0.8 broadcast_select_fusion.3
  90.9 88.2 %all-reduce.2.cloned.1.call-done = f32[3,128,2,64]{1,3,2,0:T(8,128)} async-done(((f32[3,128,2,64]{1,3,2,0:T(8,128)}), f32[3,128,2,64]{1,3,2,0:T(8,128)}) %all-reduce.2.cloned.1.call-update) | async-done | bytes 196624 | tf_op jit(solution)/shard_map/psum | solution.py:68
  179.1 1.6 convolution_bitcast_fusion
  181.1 1.9 copy-done.7
  183.0 2.0 broadcast_select_fusion.1
  185.0 1.3 fusion.48
  186.4 8.1 %fusion.4 = f32[384,1024]{1,0:T(8,128)S(1)} fusion(bf16[2,6144,1024]{2,1,0:T(8,128)(2,1)} %param.17, bf16[192,6144]{1,0:T(8,128)(2,1)S(1)} %get-tuple-element.16, bf16[192,6144]{1,0:T(8,128)(2,1)S(1)} %get-tuple-element.15), kind=kOutput, calls=%fused_computation.8 | convolution fusion | flops 4841275392 | bytes 18874368 | tf_op jit(solution)/shard_map/dot_general | solution.py:75
  194.6 10.7 %fusion.24 = bf16[384,1024]{1,0:T(8,128)(2,1)} fusion(f32[384,2,1024]{2,0,1:T(8,128)S(1)} %bitcast.66, f32[384,1024]{1,0:T(8,128)S(1)} %fusion.4, bf16[2,6144,1024]{2,1,0:T(8,128)(2,1)} %param.18, f32[384]{0:T(512)S(1)} %get-tuple-element.6, bf16[192,6144]{1,0:T(8,128)(2,1)S(1)} %get-tuple-element.16, bf16[192,6144]{1,0:T(8,128)(2,1)S(1)} %get-tuple-element.15), kind=kOutput, calls=%fused_computation.31 | convolution fusion | flops 4844814336 | bytes 21235200 | tf_op jit(solution)/shard_map/dot_general | solution.py:79
  205.6 9.5 %fusion.10 = f32[384,1024]{1,0:T(8,128)S(1)} fusion(bf16[2,6144,1024]{2,1,0:T(8,128)(2,1)} %param.17, bf16[192,6144]{1,0:T(8,128)(2,1)} %copy-done.10, bf16[192,6144]{1,0:T(8,128)(2,1)} %copy-done.8), kind=kOutput, calls=%fused_computation.14 | convolution fusion | flops 4841275392 | bytes 18874368 | tf_op jit(solution)/shard_map/dot_general | solution.py:75
  215.2 10.8 %fusion.28 = bf16[384,1024]{1,0:T(8,128)(2,1)} fusion(f32[384,2,1024]{2,0,1:T(8,128)S(1)} %bitcast.67, f32[384,1024]{1,0:T(8,128)S(1)} %fusion.10, bf16[2,6144,1024]{2,1,0:T(8,128)(2,1)} %param.18, f32[384]{0:T(512)S(1)} %get-tuple-element.5, bf16[192,6144]{1,0:T(8,128)(2,1)S(1)} %copy-done.11, bf16[192,6144]{1,0:T(8,128)(2,1)S(1)} %copy-done.9), kind=kOutput, calls=%fused_computation.36 | convolution fusion | flops 4844814336 | bytes 21235200 | tf_op jit(solution)/shard_map/dot_general | solution.py:79
  226.1 41.9 %all-gather.11.cloned.1.call-done = bf16[384,4096]{1,0:T(8,128)(2,1)} async-done(((bf16[384,1024]{1,0:T(8,128)(2,1)}), bf16[384,4096]{1,0:T(8,128)(2,1)}) %all-gather.11.cloned.1.call-update) | async-done | bytes 3145744 | tf_op jit(solution)/shard_map/all_gather | solution.py:85
  268.0 10.0 %fusion = f32[384,1536]{1,0:T(8,128)} fusion(bf16[384,4096]{1,0:T(8,128)(2,1)} %all-gather.11.cloned.1.call-done, bf16[2,4096,1536]{2,1,0:T(8,128)(2,1)} %param.19), kind=kOutput, calls=%fused_computation.4 | convolution fusion | flops 4831838208 | bytes 18087936 | tf_op jit(solution)/shard_map/dot_general | solution.py:86
  278.0 53.6 %all-gather.9.cloned.1.call-done = bf16[384,4096]{1,0:T(8,128)(2,1)} async-done(((bf16[384,1024]{1,0:T(8,128)(2,1)}), bf16[384,4096]{1,0:T(8,128)(2,1)}) %all-gather.9.cloned.1.call-update) | async-done | bytes 3145744 | tf_op jit(solution)/shard_map/all_gather | solution.py:85
  331.6 10.5 %fusion.18 = f32[384,1536]{1,0:T(8,128)} fusion(f32[384,1536]{1,0:T(8,128)} %fusion, bf16[384,4096]{1,0:T(8,128)(2,1)} %all-gather.9.cloned.1.call-done, bf16[2,4096,1536]{2,1,0:T(8,128)(2,1)} %param.19), kind=kOutput, calls=%fused_computation.23 | convolution fusion | flops 4832428032 | bytes 20447232 | tf_op jit(solution)/shard_map/dot_general | solution.py:86
  342.1 31.9 %reduce-scatter.2.cloned.1.call-done = f32[96,1536]{1,0:T(8,128)} async-done(((f32[384,1536]{1,0:T(8,128)}), f32[96,1536]{1,0:T(8,128)}) %reduce-scatter.2.cloned.1.call-update) | async-done | bytes 589840 | tf_op jit(solution)/shard_map/reduce_scatter | solution.py:88
  374.0 1.8 convert_element_type.16
  (59 shorter events, 3.2 us)
Async XLA Ops:
  6.5 83.8 %copy-start = (bf16[8,2,64,1024]{3,2,1,0:T(8,128)(2,1)S(1)}, bf16[8,2,64,1024]{3,2,1,0:T(8,128)(2,1)}, u32[]{:S(2)}) copy-start(bf16[8,2,64,1024]{3,2,1,0:T(8,128)(2,1)} %param.21) | copy-start | bytes 6291460
  6.5 78.6 %copy-start.13 = (s32[3]{0:T(128)S(1)}, s32[3]{0:T(128)}, u32[]{:S(2)}) copy-start(s32[3]{0:T(128)} %param.14) | copy-start | bytes 40
  6.5 78.6 %copy-start.2 = (s32[8]{0:T(128)S(1)}, s32[8]{0:T(128)}, u32[]{:S(2)}) copy-start(s32[8]{0:T(128)} %param.15) | copy-start | bytes 100
  6.5 24.8 %all-gather.5.cloned.1.call-start = ((), (), s32[]{:S(2)}) async-start(), calls=%async_computation.1 | async-start | bytes 1966080 | tf_op jit(solution)/shard_map/all_gather | solution.py:34
  7.3 77.9 %all-gather.7.cloned.1.call-start = ((), (), s32[]{:S(2)}) async-start(), calls=%async_computation.2 | async-start | bytes 2949120 | tf_op jit(solution)/shard_map/all_gather | solution.py:38
  33.4 52.5 %copy-start.5 = (bf16[3,128,1536]{2,1,0:T(8,128)(2,1)}, bf16[3,128,1536]{2,1,0:T(8,128)(2,1)S(1)}, u32[]{:S(2)}) copy-start(bf16[3,128,1536]{2,1,0:T(8,128)(2,1)S(1)} %gather_fusion) | copy-start | bytes 3538948
  34.5 144.6 %all-reduce.2.cloned.1.call-start = ((), (), s32[]{:S(2)}) async-start(), calls=%async_computation.3 | async-start | bytes 393216 | tf_op jit(solution)/shard_map/psum | solution.py:68
  85.1 96.0 %collective-permute-start = (bf16[192,6144]{1,0:T(8,128)(2,1)}, bf16[192,6144]{1,0:T(8,128)(2,1)}, u32[]{:S(2)}, u32[]{:S(2)}) collective-permute-start(bf16[192,6144]{1,0:T(8,128)(2,1)} %all-gather.7.cloned.1.call-done), channel_id=1, source_target_pairs={{0,4},{4,0},{1,5},{5,1},{2,6},{6,2},{3,7},{7,3},{8,12},{12,8},{9,1... | collective-permute-start | bytes 7077896 | tf_op jit(solution)/shard_map/ppermute | solution.py:39
  87.6 1.3 copy-start.6
  87.8 2.5 copy-start.12
  90.2 177.7 %all-gather.11.cloned.1.call-start = ((), (), s32[]{:S(2)}) async-start(), calls=%async_computation.5 | async-start | bytes 3932160 | tf_op jit(solution)/shard_map/all_gather | solution.py:85
  180.7 2.3 copy-start.7
  181.1 13.5 %copy-start.3 = (f32[3,128,2,1024]{3,1,0,2:T(8,128)}, f32[3,128,2,1024]{3,1,0,2:T(8,128)S(1)}, u32[]{:S(2)}) copy-start(f32[3,128,2,1024]{3,1,0,2:T(8,128)S(1)} %copy.17) | copy-start | bytes 9437188
  181.1 3.9 %copy-start.14 = (bf16[6144,8]{0,1:T(8,128)(2,1)S(1)}, bf16[6144,8]{0,1:T(8,128)(2,1)}, u32[]{:S(2)}) copy-start(bf16[6144,8]{0,1:T(8,128)(2,1)} %param.16) | copy-start | bytes 294916
  185.0 9.6 %copy-start.8 = (bf16[192,6144]{1,0:T(8,128)(2,1)}, bf16[192,6144]{1,0:T(8,128)(2,1)S(1)}, u32[]{:S(2)}) copy-start(bf16[192,6144]{1,0:T(8,128)(2,1)S(1)} %get-tuple-element.15) | copy-start | bytes 7077892
  185.0 9.6 %copy-start.10 = (bf16[192,6144]{1,0:T(8,128)(2,1)}, bf16[192,6144]{1,0:T(8,128)(2,1)S(1)}, u32[]{:S(2)}) copy-start(bf16[192,6144]{1,0:T(8,128)(2,1)S(1)} %get-tuple-element.16) | copy-start | bytes 7077892
  205.4 126.2 %all-gather.9.cloned.1.call-start = ((), (), s32[]{:S(2)}) async-start(), calls=%async_computation.4 | async-start | bytes 3932160 | tf_op jit(solution)/shard_map/all_gather | solution.py:85
  205.6 9.6 %copy-start.4 = (f32[3,128,2,1024]{3,1,0,2:T(8,128)S(1)}, f32[3,128,2,1024]{3,1,0,2:T(8,128)}, u32[]{:S(2)}) copy-start(f32[3,128,2,1024]{3,1,0,2:T(8,128)} %copy-done.3) | copy-start | bytes 9437188
  205.6 9.6 %copy-start.9 = (bf16[192,6144]{1,0:T(8,128)(2,1)S(1)}, bf16[192,6144]{1,0:T(8,128)(2,1)}, u32[]{:S(2)}) copy-start(bf16[192,6144]{1,0:T(8,128)(2,1)} %copy-done.8) | copy-start | bytes 7077892
  205.6 9.6 %copy-start.11 = (bf16[192,6144]{1,0:T(8,128)(2,1)S(1)}, bf16[192,6144]{1,0:T(8,128)(2,1)}, u32[]{:S(2)}) copy-start(bf16[192,6144]{1,0:T(8,128)(2,1)} %copy-done.10) | copy-start | bytes 7077892
  226.0 148.0 %reduce-scatter.2.cloned.1.call-start = ((), (), s32[]{:S(2)}) async-start(), calls=%async_computation.6 | async-start | bytes 2949120 | tf_op jit(solution)/shard_map/reduce_scatter | solution.py:88
  331.6 44.3 %copy-start.1 = (bf16[8,2,64,1024]{3,2,1,0:T(8,128)(2,1)S(1)}, bf16[8,2,64,1024]{3,2,1,0:T(8,128)(2,1)}, u32[]{:S(2)}) copy-start(bf16[8,2,64,1024]{3,2,1,0:T(8,128)(2,1)} %param.21) | copy-start | bytes 6291460
Sparse Core Ops, SparseCore 0:
  8.9 22.3 all-gather.4
  34.6 50.4 all-gather.6
  90.4 88.7 all-reduce.1
  205.5 62.4 all-gather.10
  269.4 62.1 all-gather.8
  342.2 31.7 reduce-scatter.1
where the time goes:
time: 383 us
  waiting for transfers between devices  290 us (76%)
  matrix products  63.1 us (16%)
  between operations  13.8 us (4%)
  local copies, waits for them, and re-layouts  8.6 us (2%)
  other arithmetic  6.66 us (2%)
    all_gather x2, waiting for transfers between devices, per_device(): gathered = lax.all_gather(hidden, 'expert', axis=1, tiled=True)  95.5 us
    psum x1, waiting for transfers between devices, per_device(): lax.psum(partial_rank, GROUP)  88.2 us
    all_gather x1, waiting for transfers between devices, per_device(): mine = lax.all_gather(mine_q, 'expert', axis=1, tiled=True)  50.6 us
    reduce_scatter x1, waiting for transfers between devices, per_device(): lax.psum_scatter(running, WIDE, scatter_dimension=0, tiled=True)  31.9 us
    all_gather x1, waiting for transfers between devices, per_device(): slots_q = lax.all_gather(prompts, WIDE, axis=0, tiled=True)  23.2 us
    dot_general x2, matrix products, per_device(): jnp.dot(input_rows, up_weight[expert_number], preferred_element_type=jnp....  21.6 us
    dot_general x2, matrix products, per_device(): jnp.dot(gathered, down_weight[expert_number], preferred_element_type=jnp....  20.5 us
    dot_general x2, matrix products, per_device(): jnp.dot(input_rows, gate_weight[expert_number], preferred_element_type=jn...  17.7 us
  transfers between devices with their start and end apart: 7, of which 6 were waited for; matrix products, arithmetic and copies ran while one was open for 10% of the time, Pallas kernels for 0%

commit v1 on v0

--- a/solution.py
+++ b/solution.py
@@ -82,7 +82,16 @@
         hidden = (weight[:, expert_number, None] * jax.nn.silu(gate_pre) * up_value).astype(
             jnp.bfloat16
         )
-        gathered = lax.all_gather(hidden, "expert", axis=1, tiled=True)
+        ways = lax.axis_size("expert")
+        up = [(d, (d + 1) % ways) for d in range(ways)]
+        down = [(d, (d - 1) % ways) for d in range(ways)]
+        earlier, later = ([hidden], [hidden])
+        for _ in range(ways // 2):
+            earlier.append(lax.ppermute(earlier[-1], "expert", up))
+        for _ in range((ways - 1) // 2):
+            later.append(lax.ppermute(later[-1], "expert", down))
+        line = jnp.concatenate([*earlier[::-1], *later[1:]], axis=1)
+        gathered = jnp.roll(line, (lax.axis_index("expert") - ways // 2) * hidden.shape[1], axis=1)
         part = jnp.dot(gathered, down_weight[expert_number], preferred_element_type=jnp.float32)
         running = part if running is None else running + part
     mixed_rows = lax.psum_scatter(running, WIDE, scatter_dimension=0, tiled=True)

time: 383 us -> 371 us (0.969)
  waiting for transfers between devices: 290 us -> 253 us
  starting transfers between devices: 0.39 us -> 22.4 us
  matrix products: 63.1 us -> 67.7 us
    all_gather x2 -> x0, waiting for transfers between devices: 95.5 us -> none  [per_device(): gathered = lax.all_gather(hidden, 'expert', axis=1, tiled=True)]
    ppermute x0 -> x6, waiting for transfers between devices: none -> 60.2 us  [the longest x4 52.1 us: per_device(): earlier.append(lax.ppermute(earlier[-1], 'expert', up))]
    ppermute x0 -> x6, starting transfers between devices: none -> 22.3 us  [the longest x4 15.2 us: per_device(): earlier.append(lax.ppermute(earlier[-1], 'expert', up))]
    dot_general x2, matrix products: 20.5 us -> 27.2 us  [per_device(): jnp.dot(gathered, down_weight[expert_number], preferred_element_type=jnp....]
  transfers between devices with their start and end apart: 7 -> 11, of which waited for: 6 -> 10; matrix products, arithmetic and copies ran while one was open for 10% -> 8% of each run, Pallas kernels for 0% -> 0%
where the time goes in v1:
time: 371 us; the launch traced here: 370 us
  waiting for transfers between devices  253 us (68%)
  matrix products  67.7 us (18%)
  starting transfers between devices  22.4 us (6%)
  between operations  13.4 us (4%)
  local copies, waits for them, and re-layouts  6.87 us (2%)
  other arithmetic  6.75 us (2%)
    psum x1, waiting for transfers between devices, per_device(): lax.psum(partial_rank, GROUP)  88.2 us
    ppermute x4, waiting for transfers between devices, per_device(): earlier.append(lax.ppermute(earlier[-1], 'expert', up))  52.1 us
    all_gather x1, waiting for transfers between devices, per_device(): mine = lax.all_gather(mine_q, 'expert', axis=1, tiled=True)  50.6 us
    reduce_scatter x1, waiting for transfers between devices, per_device(): lax.psum_scatter(running, WIDE, scatter_dimension=0, tiled=True)  30.5 us
    dot_general x2, matrix products, per_device(): jnp.dot(gathered, down_weight[expert_number], preferred_element_type=jnp....  27.2 us
    all_gather x1, waiting for transfers between devices, per_device(): slots_q = lax.all_gather(prompts, WIDE, axis=0, tiled=True)  23.2 us
    dot_general x2, matrix products, per_device(): jnp.dot(input_rows, up_weight[expert_number], preferred_element_type=jnp....  19.6 us
    dot_general x2, matrix products, per_device(): jnp.dot(input_rows, gate_weight[expert_number], preferred_element_type=jn...  16.1 us
  transfers between devices with their start and end apart: 11, of which 10 were waited for; matrix products, arithmetic and copies ran while one was open for 8% of the time, Pallas kernels for 0%

profile of v1, /device:TPU:0, one launch (start us, length us, event | category | flops | bytes accessed | tf_op | source)
XLA Modules:
  0.0 370.4 jit_solution(13584348068033215554)
XLA Ops:
  8.1 23.2 %all-gather.3.cloned.1.call-done = bf16[4,128,1536]{2,1,0:T(8,128)(2,1)} async-done(((bf16[1,128,1536]{2,1,0:T(8,128)(2,1)}), bf16[4,128,1536]{2,1,0:T(8,128)(2,1)}) %all-gather.3.cloned.1.call-update) | async-done | bytes 1572880 | tf_op jit(solution)/shard_map/all_gather | solution.py:34
  31.3 2.0 gather_fusion
  34.7 50.6 %all-gather.5.cloned.1.call-done = bf16[192,6144]{1,0:T(8,128)(2,1)} async-done(((bf16[192,1536]{1,0:T(8,128)(2,1)}), bf16[192,6144]{1,0:T(8,128)(2,1)}) %all-gather.5.cloned.1.call-update) | async-done | bytes 2359312 | tf_op jit(solution)/shard_map/all_gather | solution.py:38
  86.0 1.8 gather_fusion.3
  87.9 1.8 fusion.53
  91.2 88.2 %all-reduce.2.cloned.1.call-done = f32[3,128,2,64]{1,3,2,0:T(8,128)} async-done(((f32[3,128,2,64]{1,3,2,0:T(8,128)}), f32[3,128,2,64]{1,3,2,0:T(8,128)}) %all-reduce.2.cloned.1.call-update) | async-done | bytes 196624 | tf_op jit(solution)/shard_map/psum | solution.py:68
  182.7 2.0 broadcast_select_fusion.1
  184.7 8.0 %fusion.10 = f32[384,1024]{1,0:T(8,128)S(1)} fusion(bf16[2,6144,1024]{2,1,0:T(8,128)(2,1)} %param.19, bf16[192,6144]{1,0:T(8,128)(2,1)S(1)} %get-tuple-element.17, bf16[192,6144]{1,0:T(8,128)(2,1)S(1)} %get-tuple-element.16), kind=kOutput, calls=%fused_computation.14 | convolution fusion | flops 4841275392 | bytes 18874368 | tf_op jit(solution)/shard_map/dot_general | solution.py:75
  192.7 8.1 %fusion.4 = f32[384,1024]{1,0:T(8,128)S(1)} fusion(bf16[2,6144,1024]{2,1,0:T(8,128)(2,1)} %param.19, bf16[192,6144]{1,0:T(8,128)(2,1)S(1)} %get-tuple-element.17, bf16[192,6144]{1,0:T(8,128)(2,1)S(1)} %get-tuple-element.16), kind=kOutput, calls=%fused_computation.8 | convolution fusion | flops 4841275392 | bytes 18874368 | tf_op jit(solution)/shard_map/dot_general | solution.py:75
  202.2 9.8 %fusion.44 = bf16[384,1024]{1,0:T(8,128)(2,1)S(1)} fusion(f32[384,2,1024]{2,0,1:T(8,128)S(1)} %bitcast.64, f32[384,1024]{1,0:T(8,128)S(1)} %fusion.4, bf16[2,6144,1024]{2,1,0:T(8,128)(2,1)} %param.20, f32[384]{0:T(512)S(1)} %get-tuple-element.7, bf16[192,6144]{1,0:T(8,128)(2,1)S(1)} %get-tuple-element.17, bf16[192,6144]{1,0:T(8,128)(2,1)S(1)} %get-tuple-element.16), kind=kOutput, calls=%fused_computation.61 | convolution fusion | flops 4844814336 | bytes 21235200 | tf_op jit(solution)/shard_map/dot_general | solution.py:79
  213.7 9.8 %fusion.48 = bf16[384,1024]{1,0:T(8,128)(2,1)S(1)} fusion(f32[384,2,1024]{2,0,1:T(8,128)S(1)} %bitcast.65, f32[384,1024]{1,0:T(8,128)S(1)} %fusion.10, bf16[2,6144,1024]{2,1,0:T(8,128)(2,1)} %param.20, f32[384]{0:T(512)S(1)} %get-tuple-element.6, bf16[192,6144]{1,0:T(8,128)(2,1)S(1)} %get-tuple-element.17, bf16[192,6144]{1,0:T(8,128)(2,1)S(1)} %get-tuple-element.16), kind=kOutput, calls=%fused_computation.66 | convolution fusion | flops 4844814336 | bytes 21235200 | tf_op jit(solution)/shard_map/dot_general | solution.py:79
  224.1 3.3 collective-permute-start.6
  227.4 7.3 %collective-permute-done.4 = bf16[384,1024]{1,0:T(8,128)(2,1)S(1)} collective-permute-done((bf16[384,1024]{1,0:T(8,128)(2,1)S(1)}, bf16[384,1024]{1,0:T(8,128)(2,1)S(1)}, u32[]{:S(2)}, u32[]{:S(2)}) %collective-permute-start.4) | collective-permute-done | bytes 786464 | tf_op jit(solution)/shard_map/ppermute | solution.py:90
  234.7 3.8 %collective-permute-start.3 = (bf16[384,1024]{1,0:T(8,128)(2,1)S(1)}, bf16[384,1024]{1,0:T(8,128)(2,1)S(1)}, u32[]{:S(2)}, u32[]{:S(2)}) collective-permute-start(bf16[384,1024]{1,0:T(8,128)(2,1)S(1)} %fusion.48), channel_id=1, source_target_pairs={{0,3},{1,0},{2,1},{3,2},{4,7},{5,4},{6,5},{7,6},{8,11},{9,8},{10,9... | collective-permute-start | bytes 2359304 | tf_op jit(solution)/shard_map/ppermute | solution.py:92
  238.5 13.0 %collective-permute-done.1 = bf16[384,1024]{1,0:T(8,128)(2,1)} collective-permute-done((bf16[384,1024]{1,0:T(8,128)(2,1)S(1)}, bf16[384,1024]{1,0:T(8,128)(2,1)}, u32[]{:S(2)}, u32[]{:S(2)}) %collective-permute-start.1) | collective-permute-done | bytes 786464 | tf_op jit(solution)/shard_map/ppermute | solution.py:90
  251.5 13.0 %collective-permute-start.2 = (bf16[384,1024]{1,0:T(8,128)(2,1)}, bf16[384,1024]{1,0:T(8,128)(2,1)S(1)}, u32[]{:S(2)}, u32[]{:S(2)}) collective-permute-start(bf16[384,1024]{1,0:T(8,128)(2,1)} %collective-permute-done.1), channel_id=1, source_target_pairs={{0,1},{1,2},{2,3},{3,0},{4,5},{5,6},{6,7},{7,4},{8,9},{9,10},{10,1... | collective-permute-start | bytes 2359304 | tf_op jit(solution)/shard_map/ppermute | solution.py:90
  264.5 4.0 %collective-permute-done.6 = bf16[384,1024]{1,0:T(8,128)(2,1)} collective-permute-done((bf16[384,1024]{1,0:T(8,128)(2,1)S(1)}, bf16[384,1024]{1,0:T(8,128)(2,1)}, u32[]{:S(2)}, u32[]{:S(2)}) %collective-permute-start.6) | collective-permute-done | bytes 786464 | tf_op jit(solution)/shard_map/ppermute | solution.py:92
  268.6 16.7 %collective-permute-done.5 = bf16[384,1024]{1,0:T(8,128)(2,1)} collective-permute-done((bf16[384,1024]{1,0:T(8,128)(2,1)S(1)}, bf16[384,1024]{1,0:T(8,128)(2,1)}, u32[]{:S(2)}, u32[]{:S(2)}) %collective-permute-start.5) | collective-permute-done | bytes 786464 | tf_op jit(solution)/shard_map/ppermute | solution.py:90
  285.3 12.6 %fusion = f32[384,1536]{1,0:T(8,128)S(1)} fusion(bf16[2,4096,1536]{2,1,0:T(8,128)(2,1)} %param.21, s32[]{:T(128)S(6)} %select_n.110, bf16[384,1024]{1,0:T(8,128)(2,1)} %collective-permute-done.5, bf16[384,1024]{1,0:T(8,128)(2,1)S(1)} %collective-permute-done.4, bf16[384,1024]{1,0:T(8,128)(2,1)S(1)} %fusion.44, bf16[384,1024]{1,0:T(8,128)(2,1)} %collective-permute-done.6), kind=kOutput, calls=%fused_computation.4 | convolution fusion | flops 4857004032 | bytes 18087940 | tf_op jit(solution)/shard_map/dot_general | solution.py:95
  297.9 4.0 %collective-permute-done.3 = bf16[384,1024]{1,0:T(8,128)(2,1)S(1)} collective-permute-done((bf16[384,1024]{1,0:T(8,128)(2,1)S(1)}, bf16[384,1024]{1,0:T(8,128)(2,1)S(1)}, u32[]{:S(2)}, u32[]{:S(2)}) %collective-permute-start.3) | collective-permute-done | bytes 786464 | tf_op jit(solution)/shard_map/ppermute | solution.py:92
  301.9 15.0 %collective-permute-done.2 = bf16[384,1024]{1,0:T(8,128)(2,1)S(1)} collective-permute-done((bf16[384,1024]{1,0:T(8,128)(2,1)}, bf16[384,1024]{1,0:T(8,128)(2,1)S(1)}, u32[]{:S(2)}, u32[]{:S(2)}) %collective-permute-start.2) | collective-permute-done | bytes 786464 | tf_op jit(solution)/shard_map/ppermute | solution.py:90
  316.9 14.7 %fusion.36 = f32[384,1536]{1,0:T(8,128)} fusion(f32[384,1536]{1,0:T(8,128)S(1)} %fusion, bf16[2,4096,1536]{2,1,0:T(8,128)(2,1)} %param.21, s32[]{:T(128)S(6)} %select_n.110, bf16[384,1024]{1,0:T(8,128)(2,1)S(1)} %collective-permute-done.2, bf16[384,1024]{1,0:T(8,128)(2,1)} %collective-permute-done.1, bf16[384,1024]{1,0:T(8,128)(2,1)S(1)} %fusion.48, ...), kind=kOutput, calls=%fused_computation.53 | convolution fusion | flops 4857593856 | bytes 20447236 | tf_op jit(solution)/shard_map/dot_general | solution.py:95
  331.6 30.5 %reduce-scatter.2.cloned.1.call-done = f32[96,1536]{1,0:T(8,128)} async-done(((f32[384,1536]{1,0:T(8,128)}), f32[96,1536]{1,0:T(8,128)}) %reduce-scatter.2.cloned.1.call-update) | async-done | bytes 589840 | tf_op jit(solution)/shard_map/reduce_scatter | solution.py:97
  362.1 1.8 convert_element_type.16
  (51 shorter events, 12.1 us)
Async XLA Ops:
  6.5 84.1 %copy-start = (bf16[8,2,64,1024]{3,2,1,0:T(8,128)(2,1)S(1)}, bf16[8,2,64,1024]{3,2,1,0:T(8,128)(2,1)}, u32[]{:S(2)}) copy-start(bf16[8,2,64,1024]{3,2,1,0:T(8,128)(2,1)} %param.23) | copy-start | bytes 6291460
  6.5 78.7 %copy-start.6 = (s32[3]{0:T(128)S(1)}, s32[3]{0:T(128)}, u32[]{:S(2)}) copy-start(s32[3]{0:T(128)} %param.16) | copy-start | bytes 40
  6.5 78.7 %copy-start.2 = (s32[8]{0:T(128)S(1)}, s32[8]{0:T(128)}, u32[]{:S(2)}) copy-start(s32[8]{0:T(128)} %param.17) | copy-start | bytes 100
  6.5 24.8 %all-gather.3.cloned.1.call-start = ((), (), s32[]{:S(2)}) async-start(), calls=%async_computation.1 | async-start | bytes 1966080 | tf_op jit(solution)/shard_map/all_gather | solution.py:34
  7.3 77.9 %all-gather.5.cloned.1.call-start = ((), (), s32[]{:S(2)}) async-start(), calls=%async_computation.2 | async-start | bytes 2949120 | tf_op jit(solution)/shard_map/all_gather | solution.py:38
  33.4 52.6 %copy-start.3 = (bf16[3,128,1536]{2,1,0:T(8,128)(2,1)}, bf16[3,128,1536]{2,1,0:T(8,128)(2,1)S(1)}, u32[]{:S(2)}) copy-start(bf16[3,128,1536]{2,1,0:T(8,128)(2,1)S(1)} %gather_fusion) | copy-start | bytes 3538948
  34.6 144.8 %all-reduce.2.cloned.1.call-start = ((), (), s32[]{:S(2)}) async-start(), calls=%async_computation.3 | async-start | bytes 393216 | tf_op jit(solution)/shard_map/psum | solution.py:68
  85.2 96.2 %collective-permute-start = (bf16[192,6144]{1,0:T(8,128)(2,1)}, bf16[192,6144]{1,0:T(8,128)(2,1)}, u32[]{:S(2)}, u32[]{:S(2)}) collective-permute-start(bf16[192,6144]{1,0:T(8,128)(2,1)} %all-gather.5.cloned.1.call-done), channel_id=1, source_target_pairs={{0,4},{4,0},{1,5},{5,1},{2,6},{6,2},{3,7},{7,3},{8,12},{12,8},{9,1... | collective-permute-start | bytes 7077896 | tf_op jit(solution)/shard_map/ppermute | solution.py:39
  87.7 2.9 copy-start.5
  90.5 271.5 %reduce-scatter.2.cloned.1.call-start = ((), (), s32[]{:S(2)}) async-start(), calls=%async_computation.4 | async-start | bytes 2949120 | tf_op jit(solution)/shard_map/reduce_scatter | solution.py:97
  181.0 1.7 copy-start.4
  192.7 8.1 %copy-start.7 = (bf16[6144,8]{0,1:T(8,128)(2,1)S(1)}, bf16[6144,8]{0,1:T(8,128)(2,1)}, u32[]{:S(2)}) copy-start(bf16[6144,8]{0,1:T(8,128)(2,1)} %param.18) | copy-start | bytes 294916
  212.0 22.7 %collective-permute-start.4 = (bf16[384,1024]{1,0:T(8,128)(2,1)S(1)}, bf16[384,1024]{1,0:T(8,128)(2,1)S(1)}, u32[]{:S(2)}, u32[]{:S(2)}) collective-permute-start(bf16[384,1024]{1,0:T(8,128)(2,1)S(1)} %fusion.44), channel_id=1, source_target_pairs={{0,1},{1,2},{2,3},{3,0},{4,5},{5,6},{6,7},{7,4},{8,9},{9,10},{10,1... | collective-permute-start | bytes 2359304 | tf_op jit(solution)/shard_map/ppermute | solution.py:90
  223.5 28.1 %collective-permute-start.1 = (bf16[384,1024]{1,0:T(8,128)(2,1)S(1)}, bf16[384,1024]{1,0:T(8,128)(2,1)}, u32[]{:S(2)}, u32[]{:S(2)}) collective-permute-start(bf16[384,1024]{1,0:T(8,128)(2,1)S(1)} %fusion.48), channel_id=1, source_target_pairs={{0,1},{1,2},{2,3},{3,0},{4,5},{5,6},{6,7},{7,4},{8,9},{9,10},{10,1... | collective-permute-start | bytes 2359304 | tf_op jit(solution)/shard_map/ppermute | solution.py:90
  224.1 44.4 %collective-permute-start.6 = (bf16[384,1024]{1,0:T(8,128)(2,1)S(1)}, bf16[384,1024]{1,0:T(8,128)(2,1)}, u32[]{:S(2)}, u32[]{:S(2)}) collective-permute-start(bf16[384,1024]{1,0:T(8,128)(2,1)S(1)} %fusion.44), channel_id=1, source_target_pairs={{0,3},{1,0},{2,1},{3,2},{4,7},{5,4},{6,5},{7,6},{8,11},{9,8},{10,9... | collective-permute-start | bytes 2359304 | tf_op jit(solution)/shard_map/ppermute | solution.py:92
  234.7 50.6 %collective-permute-start.5 = (bf16[384,1024]{1,0:T(8,128)(2,1)S(1)}, bf16[384,1024]{1,0:T(8,128)(2,1)}, u32[]{:S(2)}, u32[]{:S(2)}) collective-permute-start(bf16[384,1024]{1,0:T(8,128)(2,1)S(1)} %collective-permute-done.4), channel_id=1, source_target_pairs={{0,1},{1,2},{2,3},{3,0},{4,5},{5,6},{6,7},{7,4},{8,9},{9,10},{10,1... | collective-permute-start | bytes 2359304 | tf_op jit(solution)/shard_map/ppermute | solution.py:90
  234.7 67.2 %collective-permute-start.3 = (bf16[384,1024]{1,0:T(8,128)(2,1)S(1)}, bf16[384,1024]{1,0:T(8,128)(2,1)S(1)}, u32[]{:S(2)}, u32[]{:S(2)}) collective-permute-start(bf16[384,1024]{1,0:T(8,128)(2,1)S(1)} %fusion.48), channel_id=1, source_target_pairs={{0,3},{1,0},{2,1},{3,2},{4,7},{5,4},{6,5},{7,6},{8,11},{9,8},{10,9... | collective-permute-start | bytes 2359304 | tf_op jit(solution)/shard_map/ppermute | solution.py:92
  251.5 65.4 %collective-permute-start.2 = (bf16[384,1024]{1,0:T(8,128)(2,1)}, bf16[384,1024]{1,0:T(8,128)(2,1)S(1)}, u32[]{:S(2)}, u32[]{:S(2)}) collective-permute-start(bf16[384,1024]{1,0:T(8,128)(2,1)} %collective-permute-done.1), channel_id=1, source_target_pairs={{0,1},{1,2},{2,3},{3,0},{4,5},{5,6},{6,7},{7,4},{8,9},{9,10},{10,1... | collective-permute-start | bytes 2359304 | tf_op jit(solution)/shard_map/ppermute | solution.py:90
  316.9 47.0 %copy-start.1 = (bf16[8,2,64,1024]{3,2,1,0:T(8,128)(2,1)S(1)}, bf16[8,2,64,1024]{3,2,1,0:T(8,128)(2,1)}, u32[]{:S(2)}) copy-start(bf16[8,2,64,1024]{3,2,1,0:T(8,128)(2,1)} %param.23) | copy-start | bytes 6291460
Sparse Core Ops, SparseCore 0:
  8.9 22.3 all-gather.2
  34.7 50.4 all-gather.4
  90.7 88.7 all-reduce.1
  331.7 30.3 reduce-scatter.1
